TPU v7x, 32 devices: a whole 2x2x4 slice. The times are simulated.
32 devices in a mesh: fsdp: 4 (over y, x), seq: 8 (over z, core).
Axes of the slice: x: 2, y: 2, z: 4, core: 2. Of those that a mesh axis runs over, the one named last changes fastest.
Arguments:
- events: bfloat16 [4, 1024, 2048], P('fsdp', 'seq'), may hold values from -6 to 6
- type_ids: int32 [4, 1024], P('fsdp', 'seq'), may hold values from 0 to 255
- type_table: bfloat16 [256, 2048], P('fsdp'), may hold values from -6 to 6
- norm_gain: float32 [2048], replicated, may hold values from 0.25 to 1.75
- kernel: bfloat16 [2048, 1152], P('fsdp'), may hold values from -0.1875 to 0.1875
- upstream: bfloat16 [4, 1024, 2048], P('fsdp', 'seq'), may hold values from -6 to 6
Outputs:
- input_grad: bfloat16 [4, 1024, 2048], P('fsdp', 'seq')
- table_grad: float32 [256, 2048], P(('fsdp', 'seq'))
- gain_grad: float32 [2048], P(('fsdp', 'seq'))
- kernel_grad: float32 [2048, 1152], P('seq')
All inputs are finite; a program needn't handle non-finite values.
Results may differ from a plain program's by a relative error of at most 0.0053.
Values may be sent and summed in bfloat16 or wider, within the bound.
No kernel may reach another device: no remote copies, remote signals or barrier semaphores. Data moves between devices by JAX's collectives and lax.ppermute only.
A program may use at most 128 MiB of HBM per device.

v0:
```python
import jax
import jax.numpy as jnp
from jax import lax
from jax.sharding import PartitionSpec as P

GROUPS = 16
KERNEL = 9


def with_halo(cells, sides, width):
    for axis, dim in sides:
        count = lax.axis_size(axis)
        ends = count - 1
        head = lax.slice_in_dim(cells, 0, width, axis=dim)
        tail = lax.slice_in_dim(cells, cells.shape[dim] - width, cells.shape[dim], axis=dim)
        cells = jnp.concatenate(
            [
                lax.ppermute(tail, axis, [(i, (i + 1) % count) for i in range(ends)]),
                cells,
                lax.ppermute(head, axis, [((i + 1) % count, i) for i in range(ends)]),
            ],
            axis=dim,
        )
    return cells


def from_partner(value, axis, apart):
    mask = 2**apart
    pairs = [(source, source ^ mask) for source in range(lax.axis_size(axis))]
    return lax.ppermute(value, axis, pairs)


def body(events, type_ids, type_table, norm_gain, kernel, upstream):
    length = events.shape[1]
    width = events.shape[2]
    chans = width // GROUPS
    half = KERNEL // 2
    seq_count = lax.axis_size("seq")
    total = length * seq_count * lax.axis_size("fsdp")
    scale = 1.0 / jnp.sqrt(jnp.float32(total))
    table = lax.all_gather(type_table, "fsdp", axis=0, tiled=True)
    onehot = (type_ids[0][:, None] == jnp.arange(table.shape[0], dtype=jnp.int32)[None, :]).astype(
        jnp.bfloat16
    )
    mixed = events[0].astype(jnp.float32) + jnp.dot(
        onehot, table, preferred_element_type=jnp.float32
    )
    inv = lax.rsqrt(jnp.mean(mixed * mixed, axis=-1, keepdims=True) + 1e-06)
    normed = (mixed * inv * norm_gain).astype(jnp.bfloat16)
    padded = with_halo(normed, (("seq", 0),), half)
    padded = padded.reshape(length + 2 * half, GROUPS, chans)
    weights = lax.all_gather(kernel, "fsdp", axis=0, tiled=True).reshape(
        GROUPS, chans, KERNEL, chans
    )
    conv = jnp.zeros((length, GROUPS, chans), jnp.float32)
    for k in range(KERNEL):
        conv = conv + jnp.einsum(
            "tgc,goc->tgo",
            padded[k : k + length],
            weights[:, :, k, :],
            preferred_element_type=jnp.float32,
        )
    up_float = upstream[0].astype(jnp.float32)
    sig = jax.nn.sigmoid(conv)
    dconv = (up_float.reshape(length, GROUPS, chans) * sig * (1.0 + conv * (1.0 - sig))).astype(
        jnp.bfloat16
    )
    dflat = dconv.reshape(length, width)
    dpad = with_halo(dflat, (("seq", 0),), half)
    dpad = dpad.reshape(length + 2 * half, GROUPS, chans)
    dnormed = jnp.zeros((length, GROUPS, chans), jnp.float32)
    for k in range(KERNEL):
        dnormed = dnormed + jnp.einsum(
            "tgo,goc->tgc",
            dpad[2 * half - k : 2 * half - k + length],
            weights[:, :, k, :],
            preferred_element_type=jnp.float32,
        )
    slice_width = width // seq_count
    normed_slice, dconv_slice = (
        lax.all_to_all(normed, "seq", split_axis=1, concat_axis=0, tiled=True),
        lax.all_to_all(dflat, "seq", split_axis=1, concat_axis=0, tiled=True),
    )
    whole = normed_slice.shape[0]
    if slice_width < chans:
        spread = chans // slice_width
        position = lax.axis_index("seq")
        group_rows = normed_slice
        for bit in range(spread.bit_length() - 1):
            partner = from_partner(group_rows, "seq", bit)
            lower = position >> bit & 1 == 0
            group_rows = jnp.where(
                lower,
                jnp.concatenate([group_rows, partner], axis=1),
                jnp.concatenate([partner, group_rows], axis=1),
            )
        group_in = group_rows.reshape(whole, 1, chans)
        group_out = dconv_slice.reshape(whole, 1, slice_width)
    else:
        local_groups = slice_width // chans
        group_in = normed_slice.reshape(whole, local_groups, chans)
        group_out = dconv_slice.reshape(whole, local_groups, chans)
    group_pad = jnp.pad(group_in, ((half, half), (0, 0), (0, 0)))
    kterms = []
    for k in range(KERNEL):
        kterms.append(
            jnp.einsum(
                "tgo,tgc->goc",
                group_out,
                group_pad[k : k + whole],
                preferred_element_type=jnp.float32,
            )
        )
    kernel_part = jnp.stack(kterms, axis=2).reshape(slice_width, KERNEL * chans) * scale
    kernel_grad = lax.psum(kernel_part, "fsdp")
    dnormed = dnormed.reshape(length, width)
    gain_term = jnp.sum(dnormed * mixed * inv, axis=0) * scale
    scaled = norm_gain * dnormed
    dmixed = inv * scaled - mixed * inv * inv * inv * jnp.mean(
        scaled * mixed, axis=-1, keepdims=True
    )
    input_grad = (up_float + dmixed).astype(jnp.bfloat16)
    table_term = (
        lax.dot_general(
            onehot, input_grad, (((0,), (0,)), ((), ())), preferred_element_type=jnp.float32
        )
        * scale
    )
    table_grad, gain_grad = (
        lax.psum_scatter(table_term, ("fsdp", "seq"), scatter_dimension=0, tiled=True),
        lax.psum_scatter(gain_term, ("fsdp", "seq"), scatter_dimension=0, tiled=True),
    )
    return (input_grad[None], table_grad, gain_grad, kernel_grad)


def solution(mesh):
    return jax.shard_map(
        body,
        mesh=mesh,
        in_specs=(
            P("fsdp", "seq", None),
            P("fsdp", "seq"),
            P("fsdp", None),
            P(),
            P("fsdp", None),
            P("fsdp", "seq", None),
        ),
        out_specs=(
            P("fsdp", "seq", None),
            P(("fsdp", "seq"), None),
            P(("fsdp", "seq")),
            P("seq", None),
        ),
        check_vma=False,
    )
```

profile of v0, /device:TPU:0, one launch (start us, length us, event | category | flops | bytes accessed | tf_op | source)
XLA Modules:
  0.0 384.2 jit_solution(598750002941307094)
XLA Ops:
  7.2 0.7 all-gather.3.cloned.1.call-update
  8.0 0.7 all-gather.5.cloned.1.call-update
  8.7 30.6 %all-gather.3.cloned.1.call-done = bf16[256,2048]{1,0:T(8,128)(2,1)} async-done(((bf16[64,2048]{1,0:T(8,128)(2,1)}), bf16[256,2048]{1,0:T(8,128)(2,1)}) %all-gather.3.cloned.1.call-update) | async-done | bytes 1048592 | tf_op jit(solution)/shard_map/all_gather | solution.py:41
  39.2 1.7 multiply_reduce_fusion.2
  41.1 1.0 copy.192
  42.1 4.6 %all-to-all-start.1 = ((bf16[128,8,256]{0,2,1:T(8,128)(2,1)}), bf16[128,8,256]{0,2,1:T(8,128)(2,1)S(1)}, u32[]{:S(2)}, u32[]{:S(2)}) async-start(bf16[128,8,256]{0,2,1:T(8,128)(2,1)} %bitcast.30), calls=%async_computation.2 | async-start | bytes 1048576 | tf_op jit(solution)/shard_map/all_to_all | solution.py:81
  46.7 2.4 collective-permute-start
  49.1 1.3 collective-permute-start.1
  50.6 1.2 copy.213
  51.7 1.6 collective-permute-done.1
  53.4 2.7 fusion.52
  56.0 6.0 %all-to-all-done.1 = bf16[128,8,256]{0,2,1:T(8,128)(2,1)S(1)} async-done(((bf16[128,8,256]{0,2,1:T(8,128)(2,1)}), bf16[128,8,256]{0,2,1:T(8,128)(2,1)S(1)}, u32[]{:S(2)}, u32[]{:S(2)}) %all-to-all-start.1) | async-done | bytes 524320 | tf_op jit(solution)/shard_map/all_to_all | solution.py:81
  62.6 1.0 copy.169
  63.7 34.5 %all-gather.5.cloned.1.call-done = bf16[2048,1152]{1,0:T(8,128)(2,1)} async-done(((bf16[512,1152]{1,0:T(8,128)(2,1)}), bf16[2048,1152]{1,0:T(8,128)(2,1)}) %all-gather.5.cloned.1.call-update) | async-done | bytes 4718608 | tf_op jit(solution)/shard_map/all_gather | solution.py:52
  98.2 10.5 %reshape.88 = bf16[16,128,9,128]{3,2,1,0:T(8,128)(2,1)} reshape(bf16[2048,1152]{1,0:T(8,128)(2,1)} %all-gather.5.cloned.1.call-done) | data formatting | bytes 9437184 | tf_op jit(solution)/shard_map/reshape | solution.py:52
  108.6 19.8 %fusion.82 = (bf16[16,128,1,128]{3,2,1,0:T(2,128)(2,1)S(1)}, bf16[16,128,1,128]{3,2,1,0:T(2,128)(2,1)S(1)}, bf16[16,128,1,128]{3,2,1,0:T(2,128)(2,1)S(1)}, bf16[...) fusion(bf16[16,128,9,128]{3,2,1,0:T(8,128)(2,1)} %reshape.88), kind=kLoop, calls=%fused_computation.154 | loop fusion | bytes 9437184 | tf_op jit(solution)/shard_map/slice | solution.py:60
  128.5 0.5 fusion.49
  129.0 0.9 copy-done.22
  129.9 0.5 convolution_add_fusion.15
  130.5 0.9 copy-done.21
  131.3 0.5 convolution_add_fusion.14
  131.8 0.7 copy-done.20
  132.5 0.5 convolution_add_fusion.13
  133.0 0.5 convolution_add_fusion.12
  133.6 0.5 copy-done.19
  134.1 0.5 convolution_add_fusion.11
  134.6 0.5 copy-done.18
  135.1 0.5 convolution_add_fusion.10
  135.6 0.5 convolution_add_fusion.9
  136.1 0.7 copy-done.25
  137.0 0.8 fusion.14
  137.9 1.1 copy.145
  138.9 1.3 collective-permute-start.2
  140.2 1.1 copy.155
  141.3 3.8 collective-permute-start.3
  145.1 2.7 fusion.63
  147.8 1.0 copy.144
  148.8 4.7 %all-to-all-start = ((bf16[128,8,256]{0,2,1:T(8,128)(2,1)}), bf16[128,8,256]{0,2,1:T(8,128)(2,1)S(1)}, u32[]{:S(2)}, u32[]{:S(2)}) async-start(bf16[128,8,256]{0,2,1:T(8,128)(2,1)} %bitcast.28), calls=%async_computation.1 | async-start | bytes 1048576 | tf_op jit(solution)/shard_map/all_to_all | solution.py:82
  153.7 6.9 %pad_maximum_fusion = (bf16[128,2048]{0,1:T(8,128)(2,1)S(1)}, bf16[128,2048]{0,1:T(8,128)(2,1)S(1)}, bf16[128,2048]{0,1:T(8,128)(2,1)S(1)}, bf16[128,2048]{0,1:T...) fusion(bf16[128,2048]{0,1:T(8,128)(2,1)} %bitcast.13, ...), kind=kLoop, calls=%fused_computation.105 | loop fusion | flops 8388608 | bytes 4751360 | tf_op jit(solution)/shard_map/concatenate | solution.py:16
  161.0 0.8 copy-done.7
  161.8 0.4 convolution_add_fusion.7
  162.2 0.9 copy-done.5
  163.1 0.4 convolution_add_fusion.6
  163.4 0.9 copy-done.12
  165.0 0.9 copy-done.3
  165.8 0.4 convolution_add_fusion.4
  166.2 0.9 copy-done.1
  167.4 0.4 convolution_add_fusion.2
  167.8 0.8 copy-done.15
  168.6 1.3 convolution_add_fusion.1
  170.0 1.6 copy.191
  171.5 1.1 copy.166
  172.7 1.3 reshape.83
  174.0 1.4 fusion.10
  178.0 1.9 copy.171
  180.0 2.4 copy.284
  182.7 0.7 copy-done.17
  183.4 0.4 fusion.12
  183.8 1.9 convolution_multiply_fusion
  185.7 39.9 %all-reduce.1 = f32[2048]{0:T(1024)S(1)} all-reduce(f32[2048]{0:T(1024)S(1)} %broadcast_multiply_fusion.1), channel_id=3, replica_groups=mesh['fsdp'=4,'seq'=8] {'fsdp','seq'}, use_global_device_ids=true, to_apply=%region_4.5.clone | all-reduce | flops 2048 | bytes 16384
  225.6 0.6 dynamic-slice
  226.2 11.7 %all-reduce.4.cloned.1.call-done = f32[256,1152]{0,1:T(8,128)} async-done(((f32[256,1152]{0,1:T(8,128)}), f32[256,1152]{0,1:T(8,128)}) %all-reduce.4.cloned.1.call-update) | async-done | bytes 1179664 | tf_op jit(solution)/shard_map/psum | solution.py:115
  237.9 2.7 copy.172
  240.6 137.1 %reduce-scatter.2.cloned.1.call-done = f32[8,2048]{1,0:T(8,128)} async-done(((f32[256,2048]{1,0:T(8,128)}), f32[8,2048]{1,0:T(8,128)}) %reduce-scatter.2.cloned.1.call-update) | async-done | bytes 65552 | tf_op jit(solution)/shard_map/reduce_scatter | solution.py:130
  (81 shorter events, 5.7 us)
Async XLA Ops:
  7.2 32.1 %copy-start.30 = (s32[1,128]{1,0:T(1,128)S(1)}, s32[1,128]{1,0:T(1,128)}, u32[]{:S(2)}) copy-start(s32[1,128]{1,0:T(1,128)} %param.7) | copy-start | bytes 1540
  7.2 32.1 %copy-start.26 = (bf16[1,128,2048]{2,1,0:T(8,128)(2,1)S(1)}, bf16[1,128,2048]{2,1,0:T(8,128)(2,1)}, u32[]{:S(2)}) copy-start(bf16[1,128,2048]{2,1,0:T(8,128)(2,1)} %param.6) | copy-start | bytes 1572868
  7.2 32.0 %all-gather.3.cloned.1.call-start = ((), (), s32[]{:S(2)}) async-start(), calls=%async_computation.3 | async-start | bytes 1310720 | tf_op jit(solution)/shard_map/all_gather | solution.py:41
  7.9 90.2 %all-gather.5.cloned.1.call-start = ((), (), s32[]{:S(2)}) async-start(), calls=%async_computation.4 | async-start | bytes 5898240 | tf_op jit(solution)/shard_map/all_gather | solution.py:52
  39.2 1.7 copy-start.29
  41.1 9.4 %copy-start.16 = (bf16[1,128,2048]{2,1,0:T(8,128)(2,1)S(1)}, bf16[1,128,2048]{2,1,0:T(8,128)(2,1)}, u32[]{:S(2)}) copy-start(bf16[1,128,2048]{2,1,0:T(8,128)(2,1)} %param.11) | copy-start | bytes 1572868
  42.1 20.0 %all-to-all-start.1 = ((bf16[128,8,256]{0,2,1:T(8,128)(2,1)}), bf16[128,8,256]{0,2,1:T(8,128)(2,1)S(1)}, u32[]{:S(2)}, u32[]{:S(2)}) async-start(bf16[128,8,256]{0,2,1:T(8,128)(2,1)} %bitcast.30), calls=%async_computation.2 | async-start | bytes 1048576 | tf_op jit(solution)/shard_map/all_to_all | solution.py:81
  46.7 5.0 %collective-permute-start = (bf16[4,2048]{1,0:T(4,128)(2,1)S(1)}, bf16[4,2048]{1,0:T(4,128)(2,1)S(1)}, u32[]{:S(2)}, u32[]{:S(2)}) collective-permute-start(bf16[4,2048]{1,0:T(4,128)(2,1)S(1)} %get-tuple-element.54), channel_id=1, source_target_pairs={{0,1},{1,2},{2,3},{3,4},{4,5},{5,6},{6,7},{8,9},{9,10},{10,11},{11... | collective-permute-start | bytes 49160 | tf_op jit(solution)/shard_map/ppermute | solution.py:18
  49.1 4.2 %collective-permute-start.1 = (bf16[4,2048]{1,0:T(4,128)(2,1)S(1)}, bf16[4,2048]{1,0:T(4,128)(2,1)S(1)}, u32[]{:S(2)}, u32[]{:S(2)}) collective-permute-start(bf16[4,2048]{1,0:T(4,128)(2,1)S(1)} %get-tuple-element.53), channel_id=1, source_target_pairs={{1,0},{2,1},{3,2},{4,3},{5,4},{6,5},{7,6},{9,8},{10,9},{11,10},{12... | collective-permute-start | bytes 49160 | tf_op jit(solution)/shard_map/ppermute | solution.py:20
  108.6 19.9 %copy-start.23 = (bf16[16,16,8,128]{3,2,1,0:T(8,128)(2,1)S(1)}, bf16[16,16,8,128]{3,2,1,0:T(8,128)(2,1)}, u32[]{:S(2)}) copy-start(bf16[16,16,8,128]{3,2,1,0:T(8,128)(2,1)} %get-tuple-element.51) | copy-start | bytes 1572868
  128.4 2.0 copy-start.6
  128.4 2.0 copy-start.8
  128.5 2.0 copy-start.4
  128.5 3.4 copy-start.11
  128.5 4.6 %copy-start.10 = (bf16[16,128,1,128]{3,2,1,0:T(2,128)(2,1)}, bf16[16,128,1,128]{3,2,1,0:T(2,128)(2,1)S(1)}, u32[]{:S(2)}) copy-start(bf16[16,128,1,128]{3,2,1,0:T(2,128)(2,1)S(1)} %get-tuple-element.22) | copy-start | bytes 1572868
  128.5 5.1 %copy-start.2 = (bf16[16,128,1,128]{3,2,1,0:T(2,128)(2,1)}, bf16[16,128,1,128]{3,2,1,0:T(2,128)(2,1)S(1)}, u32[]{:S(2)}) copy-start(bf16[16,128,1,128]{3,2,1,0:T(2,128)(2,1)S(1)} %get-tuple-element.21) | copy-start | bytes 1572868
  128.5 6.1 %copy-start = (bf16[16,128,1,128]{3,2,1,0:T(2,128)(2,1)}, bf16[16,128,1,128]{3,2,1,0:T(2,128)(2,1)S(1)}, u32[]{:S(2)}) copy-start(bf16[16,128,1,128]{3,2,1,0:T(2,128)(2,1)S(1)} %get-tuple-element.20) | copy-start | bytes 1572868
  128.5 7.6 %copy-start.14 = (bf16[16,128,1,128]{3,2,1,0:T(2,128)(2,1)}, bf16[16,128,1,128]{3,2,1,0:T(2,128)(2,1)S(1)}, u32[]{:S(2)}) copy-start(bf16[16,128,1,128]{3,2,1,0:T(2,128)(2,1)S(1)} %get-tuple-element.18) | copy-start | bytes 1572868
  128.5 1.4 copy-start.22
  129.9 1.4 copy-start.21
  131.3 1.2 copy-start.20
  133.0 1.0 copy-start.19
  134.1 1.0 copy-start.18
  135.6 1.2 copy-start.25
  135.6 1.3 copy-start.27
  138.9 14.8 %collective-permute-start.2 = (bf16[4,2048]{0,1:T(8,128)(2,1)}, bf16[4,2048]{0,1:T(8,128)(2,1)}, u32[]{:S(2)}, u32[]{:S(2)}) collective-permute-start(bf16[4,2048]{0,1:T(8,128)(2,1)} %copy.145), channel_id=1, source_target_pairs={{1,0},{2,1},{3,2},{4,3},{5,4},{6,5},{7,6},{9,8},{10,9},{11,10},{12... | collective-permute-start | bytes 49160 | tf_op jit(solution)/shard_map/ppermute | solution.py:20
  141.3 12.4 %collective-permute-start.3 = (bf16[4,2048]{0,1:T(8,128)(2,1)}, bf16[4,2048]{0,1:T(8,128)(2,1)}, u32[]{:S(2)}, u32[]{:S(2)}) collective-permute-start(bf16[4,2048]{0,1:T(8,128)(2,1)} %copy.155), channel_id=1, source_target_pairs={{0,1},{1,2},{2,3},{3,4},{4,5},{5,6},{6,7},{8,9},{9,10},{10,11},{11... | collective-permute-start | bytes 49160 | tf_op jit(solution)/shard_map/ppermute | solution.py:18
  148.8 22.7 %all-to-all-start = ((bf16[128,8,256]{0,2,1:T(8,128)(2,1)}), bf16[128,8,256]{0,2,1:T(8,128)(2,1)S(1)}, u32[]{:S(2)}, u32[]{:S(2)}) async-start(bf16[128,8,256]{0,2,1:T(8,128)(2,1)} %bitcast.28), calls=%async_computation.1 | async-start | bytes 1048576 | tf_op jit(solution)/shard_map/all_to_all | solution.py:82
  153.5 84.4 %all-reduce.4.cloned.1.call-start = ((), (), s32[]{:S(2)}) async-start(), calls=%async_computation.6 | async-start | bytes 2359296 | tf_op jit(solution)/shard_map/psum | solution.py:115
  153.7 6.9 %copy-start.9 = (bf16[16,128,1,128]{3,2,1,0:T(2,128)(2,1)S(1)}, bf16[16,128,1,128]{3,2,1,0:T(2,128)(2,1)}, u32[]{:S(2)}) copy-start(bf16[16,128,1,128]{3,2,1,0:T(2,128)(2,1)} %copy-done.8) | copy-start | bytes 1572868
  160.6 1.2 copy-start.7
  161.8 1.2 copy-start.5
  163.1 1.2 copy-start.12
  163.1 1.5 copy-start.13
  164.6 1.2 copy-start.3
  165.8 1.2 copy-start.1
  167.4 1.2 copy-start.15
  173.9 1.4 copy-start.28
  182.3 1.0 copy-start.17
  182.4 195.3 %reduce-scatter.2.cloned.1.call-start = ((), (), s32[]{:S(2)}) async-start(), calls=%async_computation.5 | async-start | bytes 2162688 | tf_op jit(solution)/shard_map/reduce_scatter | solution.py:130
  183.8 1.9 copy-start.24
Sparse Core Ops, SparseCore 0:
  9.9 29.3 all-gather.2
  41.1 57.0 all-gather.4
  182.5 55.3 all-reduce.3
  240.7 136.9 reduce-scatter.1
where the time goes:
time: 386 us; the launch traced here: 384 us
  waiting for transfers between devices  223 us (58%)
  local copies, waits for them, and re-layouts  59.2 us (15%)
  blocking collectives  39.9 us (10%)
  matrix products  18.8 us (5%)
  starting transfers between devices  18.4 us (5%)
  between operations  14.4 us (4%)
  other arithmetic  10.6 us (3%)
    reduce_scatter x1, waiting for transfers between devices, body(): lax.psum_scatter(table_term, ('fsdp', 'seq'), scatter_dimension=0, tiled=...  137 us
    unnamed x1, blocking collectives  39.9 us
    all_gather x1, waiting for transfers between devices, body(): lax.all_gather(kernel, 'fsdp', axis=0, tiled=True)  34.5 us
    all_gather x1, waiting for transfers between devices, body(): table = lax.all_gather(type_table, 'fsdp', axis=0, tiled=True)  30.6 us
    slice x1, local copies, waits for them, and re-layouts, body(): weights[:, :, k, :]  19.8 us
    unnamed x66, local copies, waits for them, and re-layouts  17.4 us
    psum x1, waiting for transfers between devices, body(): kernel_grad = lax.psum(kernel_part, 'fsdp')  11.7 us
    reshape x1, local copies, waits for them, and re-layouts, body(): lax.all_gather(kernel, 'fsdp', axis=0, tiled=True)  10.5 us
  transfers between devices with their start and end apart: 10, of which 6 were waited for; matrix products, arithmetic and copies ran while one was open for 8% of the time, Pallas kernels for 0%

commit v1 on v0

--- a/solution.py
+++ b/solution.py
@@ -38,7 +38,12 @@
     seq_count = lax.axis_size("seq")
     total = length * seq_count * lax.axis_size("fsdp")
     scale = 1.0 / jnp.sqrt(jnp.float32(total))
-    table = lax.all_gather(type_table, "fsdp", axis=0, tiled=True)
+    ring = [type_table]
+    for hop in range(3):
+        ring.append(lax.ppermute(ring[-1], "fsdp", [(dev, (dev + 1) % 4) for dev in range(4)]))
+    table = jnp.roll(
+        jnp.concatenate(ring[::-1], axis=0), (lax.axis_index("fsdp") + 1) * ring[0].shape[0], axis=0
+    )
     onehot = (type_ids[0][:, None] == jnp.arange(table.shape[0], dtype=jnp.int32)[None, :]).astype(
         jnp.bfloat16
     )

time: 386 us -> 365 us (0.946)
  waiting for transfers between devices: 223 us -> 197 us
  starting transfers between devices: 18.4 us -> 23.3 us
    ppermute x0 -> x3, waiting for transfers between devices: none -> 32.1 us  [body(): lax.ppermute(ring[-1], 'fsdp', [(dev, (dev + 1) % 4) for dev in range(4)])]
    all_gather x1 -> x0, waiting for transfers between devices: 30.6 us -> none  [body(): table = lax.all_gather(type_table, 'fsdp', axis=0, tiled=True)]
    all_gather x1, waiting for transfers between devices: 34.5 us -> 7.95 us  [body(): lax.all_gather(kernel, 'fsdp', axis=0, tiled=True)]
    ppermute x0 -> x3, starting transfers between devices: none -> 4.77 us  [body(): lax.ppermute(ring[-1], 'fsdp', [(dev, (dev + 1) % 4) for dev in range(4)])]
    unnamed x66 -> x75, local copies, waits for them, and re-layouts: 17.4 us -> 18.9 us
  transfers between devices with their start and end apart: 10 -> 12, of which waited for: 6 -> 8; matrix products, arithmetic and copies ran while one was open for 8% -> 8% of each run, Pallas kernels for 0% -> 0%
where the time goes in v1:
time: 365 us; the launch traced here: 363 us
  waiting for transfers between devices  197 us (54%)
  local copies, waits for them, and re-layouts  60.1 us (16%)
  blocking collectives  39.9 us (11%)
  starting transfers between devices  23.3 us (6%)
  matrix products  17.5 us (5%)
  between operations  14.4 us (4%)
  other arithmetic  10.6 us (3%)
    reduce_scatter x1, waiting for transfers between devices, body(): lax.psum_scatter(table_term, ('fsdp', 'seq'), scatter_dimension=0, tiled=...  137 us
    unnamed x1, blocking collectives  39.9 us
    ppermute x3, waiting for transfers between devices, body(): lax.ppermute(ring[-1], 'fsdp', [(dev, (dev + 1) % 4) for dev in range(4)])  32.1 us
    slice x1, local copies, waits for them, and re-layouts, body(): weights[:, :, k, :]  19.2 us
    unnamed x75, local copies, waits for them, and re-layouts  18.9 us
    psum x1, waiting for transfers between devices, body(): kernel_grad = lax.psum(kernel_part, 'fsdp')  11.7 us
    reshape x1, local copies, waits for them, and re-layouts, body(): lax.all_gather(kernel, 'fsdp', axis=0, tiled=True)  10.5 us
    all_gather x1, waiting for transfers between devices, body(): lax.all_gather(kernel, 'fsdp', axis=0, tiled=True)  7.95 us
  transfers between devices with their start and end apart: 12, of which 8 were waited for; matrix products, arithmetic and copies ran while one was open for 8% of the time, Pallas kernels for 0%

profile of v1, /device:TPU:0, one launch (start us, length us, event | category | flops | bytes accessed | tf_op | source)
XLA Modules:
  0.0 363.0 jit_solution(13792615873049394136)
XLA Ops:
  7.2 0.7 all-gather.2.cloned.1.call-update
  8.1 2.9 collective-permute-start
  11.1 7.3 %collective-permute-done = bf16[64,2048]{1,0:T(8,128)(2,1)S(1)} collective-permute-done((bf16[64,2048]{1,0:T(8,128)(2,1)S(1)}, bf16[64,2048]{1,0:T(8,128)(2,1)S(1)}, u32[]{:S(2)}, u32[]{:S(2)}) %collective-permute-start) | collective-permute-done | bytes 262176 | tf_op jit(solution)/shard_map/ppermute | solution.py:43
  18.3 0.8 collective-permute-start.1
  19.1 12.4 %collective-permute-done.1 = bf16[64,2048]{1,0:T(8,128)(2,1)S(1)} collective-permute-done((bf16[64,2048]{1,0:T(8,128)(2,1)S(1)}, bf16[64,2048]{1,0:T(8,128)(2,1)S(1)}, u32[]{:S(2)}, u32[]{:S(2)}) %collective-permute-start.1) | collective-permute-done | bytes 262176 | tf_op jit(solution)/shard_map/ppermute | solution.py:43
  31.5 1.0 collective-permute-start.2
  32.6 12.4 %collective-permute-done.2 = bf16[64,2048]{1,0:T(8,128)(2,1)S(1)} collective-permute-done((bf16[64,2048]{1,0:T(8,128)(2,1)S(1)}, bf16[64,2048]{1,0:T(8,128)(2,1)S(1)}, u32[]{:S(2)}, u32[]{:S(2)}) %collective-permute-start.2) | collective-permute-done | bytes 262176 | tf_op jit(solution)/shard_map/ppermute | solution.py:43
  45.2 0.9 copy-done.29
  46.1 0.4 multiply_reduce_fusion.2
  47.0 1.0 copy.192
  48.0 4.8 %all-to-all-start.1 = ((bf16[128,8,256]{0,2,1:T(8,128)(2,1)}), bf16[128,8,256]{0,2,1:T(8,128)(2,1)S(1)}, u32[]{:S(2)}, u32[]{:S(2)}) async-start(bf16[128,8,256]{0,2,1:T(8,128)(2,1)} %bitcast.30), calls=%async_computation.2 | async-start | bytes 1048576 | tf_op jit(solution)/shard_map/all_to_all | solution.py:86
  52.8 2.4 collective-permute-start.3
  55.2 1.3 collective-permute-start.4
  56.6 1.2 copy.213
  57.8 1.6 collective-permute-done.4
  59.4 2.7 fusion.53
  62.1 6.0 %all-to-all-done.1 = bf16[128,8,256]{0,2,1:T(8,128)(2,1)S(1)} async-done(((bf16[128,8,256]{0,2,1:T(8,128)(2,1)}), bf16[128,8,256]{0,2,1:T(8,128)(2,1)S(1)}, u32[]{:S(2)}, u32[]{:S(2)}) %all-to-all-start.1) | async-done | bytes 524320 | tf_op jit(solution)/shard_map/all_to_all | solution.py:86
  68.7 1.0 copy.169
  69.7 8.0 %all-gather.2.cloned.1.call-done = bf16[2048,1152]{1,0:T(8,128)(2,1)} async-done(((bf16[512,1152]{1,0:T(8,128)(2,1)}), bf16[2048,1152]{1,0:T(8,128)(2,1)}) %all-gather.2.cloned.1.call-update) | async-done | bytes 4718608 | tf_op jit(solution)/shard_map/all_gather | solution.py:57
  77.6 10.5 %reshape.88 = bf16[16,128,9,128]{3,2,1,0:T(8,128)(2,1)} reshape(bf16[2048,1152]{1,0:T(8,128)(2,1)} %all-gather.2.cloned.1.call-done) | data formatting | bytes 9437184 | tf_op jit(solution)/shard_map/reshape | solution.py:57
  88.1 19.2 %fusion.84 = (bf16[16,128,1,128]{3,2,1,0:T(2,128)(2,1)S(1)}, bf16[16,128,1,128]{3,2,1,0:T(2,128)(2,1)S(1)}, bf16[16,128,1,128]{3,2,1,0:T(2,128)(2,1)S(1)}, bf16[...) fusion(bf16[16,128,9,128]{3,2,1,0:T(8,128)(2,1)} %reshape.88), kind=kLoop, calls=%fused_computation.164 | loop fusion | bytes 9437184 | tf_op jit(solution)/shard_map/slice | solution.py:65
  107.4 0.5 fusion.50
  107.9 0.9 copy-done.22
  108.8 0.5 convolution_add_fusion.15
  109.3 0.9 copy-done.21
  110.2 0.5 convolution_add_fusion.14
  110.7 0.7 copy-done.20
  111.4 0.5 convolution_add_fusion.13
  111.9 0.5 convolution_add_fusion.12
  112.5 0.5 copy-done.19
  112.9 0.5 convolution_add_fusion.11
  113.4 0.5 copy-done.18
  114.0 0.5 convolution_add_fusion.10
  114.5 0.5 convolution_add_fusion.9
  115.0 0.7 copy-done.25
  115.8 0.8 fusion.14
  116.7 1.0 copy.145
  117.8 1.3 collective-permute-start.5
  119.0 1.1 copy.155
  120.1 3.8 %collective-permute-start.6 = (bf16[4,2048]{0,1:T(8,128)(2,1)}, bf16[4,2048]{0,1:T(8,128)(2,1)}, u32[]{:S(2)}, u32[]{:S(2)}) collective-permute-start(bf16[4,2048]{0,1:T(8,128)(2,1)} %copy.155), channel_id=1, source_target_pairs={{0,1},{1,2},{2,3},{3,4},{4,5},{5,6},{6,7},{8,9},{9,10},{10,11},{11... | collective-permute-start | bytes 49160 | tf_op jit(solution)/shard_map/ppermute | solution.py:18
  124.0 2.7 fusion.64
  126.7 1.0 copy.144
  127.7 4.6 %all-to-all-start = ((bf16[128,8,256]{0,2,1:T(8,128)(2,1)}), bf16[128,8,256]{0,2,1:T(8,128)(2,1)S(1)}, u32[]{:S(2)}, u32[]{:S(2)}) async-start(bf16[128,8,256]{0,2,1:T(8,128)(2,1)} %bitcast.28), calls=%async_computation.1 | async-start | bytes 1048576 | tf_op jit(solution)/shard_map/all_to_all | solution.py:87
  132.6 6.8 %pad_maximum_fusion = (bf16[128,2048]{0,1:T(8,128)(2,1)S(1)}, bf16[128,2048]{0,1:T(8,128)(2,1)S(1)}, bf16[128,2048]{0,1:T(8,128)(2,1)S(1)}, bf16[128,2048]{0,1:T...) fusion(bf16[128,2048]{0,1:T(8,128)(2,1)} %bitcast.13, ...), kind=kLoop, calls=%fused_computation.106 | loop fusion | flops 8388608 | bytes 4751360 | tf_op jit(solution)/shard_map/concatenate | solution.py:16
  139.8 0.8 copy-done.7
  141.0 0.9 copy-done.5
  142.2 0.9 copy-done.12
  143.8 0.9 copy-done.3
  145.0 0.9 copy-done.1
  146.6 0.9 copy-done.15
  147.5 1.3 convolution_add_fusion.1
  148.8 1.6 copy.191
  150.4 1.1 copy.166
  151.5 1.3 reshape.83
  152.8 1.4 fusion.10
  156.9 1.9 copy.171
  158.8 2.4 copy.284
  161.5 0.7 copy-done.17
  162.6 1.9 convolution_multiply_fusion
  164.6 39.9 %all-reduce.1 = f32[2048]{0:T(1024)S(1)} all-reduce(f32[2048]{0:T(1024)S(1)} %broadcast_multiply_fusion.1), channel_id=3, replica_groups=mesh['fsdp'=4,'seq'=8] {'fsdp','seq'}, use_global_device_ids=true, to_apply=%region_4.5.clone | all-reduce | flops 2048 | bytes 16384
  204.4 0.6 dynamic-slice
  205.0 11.7 %all-reduce.4.cloned.1.call-done = f32[256,1152]{0,1:T(8,128)} async-done(((f32[256,1152]{0,1:T(8,128)}), f32[256,1152]{0,1:T(8,128)}) %all-reduce.4.cloned.1.call-update) | async-done | bytes 1179664 | tf_op jit(solution)/shard_map/psum | solution.py:120
  216.7 2.7 copy.172
  219.4 137.1 %reduce-scatter.2.cloned.1.call-done = f32[8,2048]{1,0:T(8,128)} async-done(((f32[256,2048]{1,0:T(8,128)}), f32[8,2048]{1,0:T(8,128)}) %reduce-scatter.2.cloned.1.call-update) | async-done | bytes 65552 | tf_op jit(solution)/shard_map/reduce_scatter | solution.py:135
  (94 shorter events, 8.1 us)
Async XLA Ops:
  7.2 1.0 copy-start.26
  7.2 70.5 %all-gather.2.cloned.1.call-start = ((), (), s32[]{:S(2)}) async-start(), calls=%async_computation.3 | async-start | bytes 5898240 | tf_op jit(solution)/shard_map/all_gather | solution.py:57
  8.1 10.2 %collective-permute-start = (bf16[64,2048]{1,0:T(8,128)(2,1)S(1)}, bf16[64,2048]{1,0:T(8,128)(2,1)S(1)}, u32[]{:S(2)}, u32[]{:S(2)}) collective-permute-start(bf16[64,2048]{1,0:T(8,128)(2,1)S(1)} %copy-done.26), channel_id=1, source_target_pairs={{0,8},{8,16},{16,24},{24,0},{1,9},{9,17},{17,25},{25,1},{2,10},{10... | collective-permute-start | bytes 786440 | tf_op jit(solution)/shard_map/ppermute | solution.py:43
  18.3 13.2 %collective-permute-start.1 = (bf16[64,2048]{1,0:T(8,128)(2,1)S(1)}, bf16[64,2048]{1,0:T(8,128)(2,1)S(1)}, u32[]{:S(2)}, u32[]{:S(2)}) collective-permute-start(bf16[64,2048]{1,0:T(8,128)(2,1)S(1)} %collective-permute-done), channel_id=1, source_target_pairs={{0,8},{8,16},{16,24},{24,0},{1,9},{9,17},{17,25},{25,1},{2,10},{10... | collective-permute-start | bytes 786440 | tf_op jit(solution)/shard_map/ppermute | solution.py:43
  31.5 13.4 %collective-permute-start.2 = (bf16[64,2048]{1,0:T(8,128)(2,1)S(1)}, bf16[64,2048]{1,0:T(8,128)(2,1)S(1)}, u32[]{:S(2)}, u32[]{:S(2)}) collective-permute-start(bf16[64,2048]{1,0:T(8,128)(2,1)S(1)} %collective-permute-done.1), channel_id=1, source_target_pairs={{0,8},{8,16},{16,24},{24,0},{1,9},{9,17},{17,25},{25,1},{2,10},{10... | collective-permute-start | bytes 786440 | tf_op jit(solution)/shard_map/ppermute | solution.py:43
  45.1 1.0 copy-start.29
  45.1 1.0 copy-start.31
  46.1 0.7 copy-start.30
  47.0 9.5 %copy-start.16 = (bf16[1,128,2048]{2,1,0:T(8,128)(2,1)S(1)}, bf16[1,128,2048]{2,1,0:T(8,128)(2,1)}, u32[]{:S(2)}) copy-start(bf16[1,128,2048]{2,1,0:T(8,128)(2,1)} %param.11) | copy-start | bytes 1572868
  48.0 20.1 %all-to-all-start.1 = ((bf16[128,8,256]{0,2,1:T(8,128)(2,1)}), bf16[128,8,256]{0,2,1:T(8,128)(2,1)S(1)}, u32[]{:S(2)}, u32[]{:S(2)}) async-start(bf16[128,8,256]{0,2,1:T(8,128)(2,1)} %bitcast.30), calls=%async_computation.2 | async-start | bytes 1048576 | tf_op jit(solution)/shard_map/all_to_all | solution.py:86
  52.8 5.0 %collective-permute-start.3 = (bf16[4,2048]{1,0:T(4,128)(2,1)S(1)}, bf16[4,2048]{1,0:T(4,128)(2,1)S(1)}, u32[]{:S(2)}, u32[]{:S(2)}) collective-permute-start(bf16[4,2048]{1,0:T(4,128)(2,1)S(1)} %get-tuple-element.54), channel_id=1, source_target_pairs={{0,1},{1,2},{2,3},{3,4},{4,5},{5,6},{6,7},{8,9},{9,10},{10,11},{11... | collective-permute-start | bytes 49160 | tf_op jit(solution)/shard_map/ppermute | solution.py:18
  55.2 4.2 %collective-permute-start.4 = (bf16[4,2048]{1,0:T(4,128)(2,1)S(1)}, bf16[4,2048]{1,0:T(4,128)(2,1)S(1)}, u32[]{:S(2)}, u32[]{:S(2)}) collective-permute-start(bf16[4,2048]{1,0:T(4,128)(2,1)S(1)} %get-tuple-element.53), channel_id=1, source_target_pairs={{1,0},{2,1},{3,2},{4,3},{5,4},{6,5},{7,6},{9,8},{10,9},{11,10},{12... | collective-permute-start | bytes 49160 | tf_op jit(solution)/shard_map/ppermute | solution.py:20
  88.1 19.3 %copy-start.23 = (bf16[16,16,8,128]{3,2,1,0:T(8,128)(2,1)S(1)}, bf16[16,16,8,128]{3,2,1,0:T(8,128)(2,1)}, u32[]{:S(2)}) copy-start(bf16[16,16,8,128]{3,2,1,0:T(8,128)(2,1)} %get-tuple-element.51) | copy-start | bytes 1572868
  107.3 2.0 copy-start.6
  107.3 2.0 copy-start.8
  107.3 2.0 copy-start.4
  107.3 3.4 copy-start.11
  107.3 4.6 %copy-start.10 = (bf16[16,128,1,128]{3,2,1,0:T(2,128)(2,1)}, bf16[16,128,1,128]{3,2,1,0:T(2,128)(2,1)S(1)}, u32[]{:S(2)}) copy-start(bf16[16,128,1,128]{3,2,1,0:T(2,128)(2,1)S(1)} %get-tuple-element.22) | copy-start | bytes 1572868
  107.3 5.1 %copy-start.2 = (bf16[16,128,1,128]{3,2,1,0:T(2,128)(2,1)}, bf16[16,128,1,128]{3,2,1,0:T(2,128)(2,1)S(1)}, u32[]{:S(2)}) copy-start(bf16[16,128,1,128]{3,2,1,0:T(2,128)(2,1)S(1)} %get-tuple-element.21) | copy-start | bytes 1572868
  107.3 6.1 %copy-start = (bf16[16,128,1,128]{3,2,1,0:T(2,128)(2,1)}, bf16[16,128,1,128]{3,2,1,0:T(2,128)(2,1)S(1)}, u32[]{:S(2)}) copy-start(bf16[16,128,1,128]{3,2,1,0:T(2,128)(2,1)S(1)} %get-tuple-element.20) | copy-start | bytes 1572868
  107.4 7.6 %copy-start.14 = (bf16[16,128,1,128]{3,2,1,0:T(2,128)(2,1)}, bf16[16,128,1,128]{3,2,1,0:T(2,128)(2,1)S(1)}, u32[]{:S(2)}) copy-start(bf16[16,128,1,128]{3,2,1,0:T(2,128)(2,1)S(1)} %get-tuple-element.18) | copy-start | bytes 1572868
  107.4 1.4 copy-start.22
  108.8 1.4 copy-start.21
  110.2 1.2 copy-start.20
  111.9 1.0 copy-start.19
  112.9 1.0 copy-start.18
  114.5 1.2 copy-start.25
  114.5 1.3 copy-start.27
  117.8 14.8 %collective-permute-start.5 = (bf16[4,2048]{0,1:T(8,128)(2,1)}, bf16[4,2048]{0,1:T(8,128)(2,1)}, u32[]{:S(2)}, u32[]{:S(2)}) collective-permute-start(bf16[4,2048]{0,1:T(8,128)(2,1)} %copy.145), channel_id=1, source_target_pairs={{1,0},{2,1},{3,2},{4,3},{5,4},{6,5},{7,6},{9,8},{10,9},{11,10},{12... | collective-permute-start | bytes 49160 | tf_op jit(solution)/shard_map/ppermute | solution.py:20
  120.1 12.4 %collective-permute-start.6 = (bf16[4,2048]{0,1:T(8,128)(2,1)}, bf16[4,2048]{0,1:T(8,128)(2,1)}, u32[]{:S(2)}, u32[]{:S(2)}) collective-permute-start(bf16[4,2048]{0,1:T(8,128)(2,1)} %copy.155), channel_id=1, source_target_pairs={{0,1},{1,2},{2,3},{3,4},{4,5},{5,6},{6,7},{8,9},{9,10},{10,11},{11... | collective-permute-start | bytes 49160 | tf_op jit(solution)/shard_map/ppermute | solution.py:18
  127.7 22.7 %all-to-all-start = ((bf16[128,8,256]{0,2,1:T(8,128)(2,1)}), bf16[128,8,256]{0,2,1:T(8,128)(2,1)S(1)}, u32[]{:S(2)}, u32[]{:S(2)}) async-start(bf16[128,8,256]{0,2,1:T(8,128)(2,1)} %bitcast.28), calls=%async_computation.1 | async-start | bytes 1048576 | tf_op jit(solution)/shard_map/all_to_all | solution.py:87
  132.3 84.4 %all-reduce.4.cloned.1.call-start = ((), (), s32[]{:S(2)}) async-start(), calls=%async_computation.5 | async-start | bytes 2359296 | tf_op jit(solution)/shard_map/psum | solution.py:120
  132.6 6.9 %copy-start.9 = (bf16[16,128,1,128]{3,2,1,0:T(2,128)(2,1)S(1)}, bf16[16,128,1,128]{3,2,1,0:T(2,128)(2,1)}, u32[]{:S(2)}) copy-start(bf16[16,128,1,128]{3,2,1,0:T(2,128)(2,1)} %copy-done.8) | copy-start | bytes 1572868
  139.4 1.2 copy-start.7
  140.7 1.2 copy-start.5
  141.9 1.2 copy-start.12
  141.9 1.5 copy-start.13
  143.4 1.2 copy-start.3
  144.6 1.2 copy-start.1
  146.2 1.2 copy-start.15
  152.8 1.4 copy-start.28
  161.2 1.0 copy-start.17
  161.2 195.3 %reduce-scatter.2.cloned.1.call-start = ((), (), s32[]{:S(2)}) async-start(), calls=%async_computation.4 | async-start | bytes 2162688 | tf_op jit(solution)/shard_map/reduce_scatter | solution.py:135
  162.6 1.9 copy-start.24
Sparse Core Ops, SparseCore 0:
  9.8 67.7 all-gather.1
  161.3 55.4 all-reduce.3
  219.7 136.7 reduce-scatter.1
